TPU v7x, 512 devices: a whole 4x4x16 slice. The times are simulated.
512 devices in a mesh: seq: 128 (over y, z, core), head: 4 (over x).
Axes of the slice: x: 4, y: 4, z: 16, core: 2. Of those that a mesh axis runs over, the one named last changes fastest.
Arguments:
- tokens: bfloat16 [64, 4, 1024], P('head'), may hold values from -6 to 6
- cache_keys: bfloat16 [64, 4096, 512], P(None, 'seq', 'head'), may hold values from -70 to 70
- cache_values: bfloat16 [64, 4096, 512], P(None, 'seq', 'head'), may hold values from -6 to 6
- held_states: bfloat16 [64, 512, 1024], P(None, 'seq'), may hold values from -6 to 6
- recompute_pos: int32 [64, 512], P(None, 'seq'), may hold values from 0 to 4095, as said below
- cache_len: int32 [64], replicated, may hold values from 1 to 4096
- new_prompt: int32 [64], replicated, may hold values 0 or 1
- w_qkv: bfloat16 [3, 1024, 512], P(None, None, 'head'), may hold values from -0.1875 to 0.1875
- qkv_bias: float32 [3, 512], P(None, 'head'), may hold values from -3 to 3
- w_out: bfloat16 [512, 1024], P('head'), may hold values from -1.5 to 1.5
- out_bias: float32 [1024], replicated, may hold values from -3 to 3
- attn_gain: float32 [1024], replicated, may hold values from 0.1 to 1.9
- attn_shift: float32 [1024], replicated, may hold values from -3 to 3
- w_up: bfloat16 [1024, 2048], P(None, 'head'), may hold values from -0.1875 to 0.1875
- up_bias: float32 [2048], P('head'), may hold values from -3 to 3
- w_down: bfloat16 [2048, 1024], P('head'), may hold values from -0.125 to 0.125
- down_bias: float32 [1024], replicated, may hold values from -3 to 3
- ffn_gain: float32 [1024], replicated, may hold values from 0.1 to 1.9
- ffn_shift: float32 [1024], replicated, may hold values from -3 to 3
Outputs:
- layer_out: bfloat16 [64, 4, 1024], P('head')
Inputs may be any that keep to these rules, and one draw needn't show every extreme that they name: `recompute_pos`: columns s * 4 to (s + 1) * 4 - 1 of a row hold distinct positions from s * 32 to (s + 1) * 32 - 1.
All inputs are finite; a program needn't handle non-finite values.
Results may differ from a plain program's by a relative error of at most 0.011.
Values may be sent and summed in bfloat16 or wider, within the bound.
No kernel may reach another device: no remote copies, remote signals or barrier semaphores. Data moves between devices by JAX's collectives and lax.ppermute only.
A program may use at most 192 MiB of HBM per device.

v0:
```python
import jax
import jax.numpy as jnp
from jax import lax
from jax.sharding import PartitionSpec as P

HDIM = 64
NEG = -1e30
EPS = 1e-05


def layer_norm(values, norm_gain, norm_bias):
    center = jnp.mean(values, axis=-1, keepdims=True)
    spread = values - center
    second = jnp.mean(spread * spread, axis=-1, keepdims=True)
    return spread * lax.rsqrt(second + EPS) * norm_gain + norm_bias


def merge_pair(first_part, second_part):
    first_max, first_sum, first_out = first_part
    second_max, second_sum, second_out = second_part
    joint_max = jnp.maximum(first_max, second_max)
    first_scale = jnp.exp(first_max - joint_max)
    second_scale = jnp.exp(second_max - joint_max)
    return (
        joint_max,
        first_sum * first_scale + second_sum * second_scale,
        first_out * first_scale[..., None] + second_out * second_scale[..., None],
    )


def partial_attention(queries, keys_here, values_here, visible):
    scores = jnp.einsum(
        "rthe,rphe->rthp", queries, keys_here, preferred_element_type=jnp.float32
    ) * HDIM ** (-0.5)
    highest = jnp.max(jnp.where(visible, scores, NEG), axis=-1)
    weights = jnp.exp(jnp.where(visible, scores - highest[..., None], NEG)).astype(jnp.bfloat16)
    totals = jnp.sum(weights.astype(jnp.float32), axis=-1)
    blended = jnp.einsum(
        "rthp,rphe->rthe", weights, values_here, preferred_element_type=jnp.float32
    )
    return (highest, totals, blended)


def seq_merge(block_max, block_sum, block_out):
    n_seq = lax.axis_size("seq")
    head_shape = block_out.shape
    lanes = head_shape[-2] * head_shape[-1]
    rows = block_out.size // lanes
    stat_rows = block_max.size // lanes
    out2 = block_out.reshape(rows, lanes)
    top = block_max.reshape(stat_rows, lanes)
    total = block_sum.reshape(stat_rows, lanes)
    width = head_shape[-1]
    step = 1
    while step < n_seq:
        pairs = [(i, i ^ step) for i in range(n_seq)]
        packed = jnp.concatenate([out2, top, total], axis=0)
        other = lax.ppermute(packed, "seq", pairs)
        o_out = other[:rows]
        o_top = other[rows : rows + stat_rows]
        o_total = other[rows + stat_rows :]
        joint = jnp.maximum(top, o_top)
        mine = jnp.exp(top - joint)
        theirs = jnp.exp(o_top - joint)
        total = total * mine + o_total * theirs
        mine_rows = jnp.repeat(mine.reshape(rows, lanes // width), width, axis=1)
        theirs_rows = jnp.repeat(theirs.reshape(rows, lanes // width), width, axis=1)
        out2 = out2 * mine_rows + o_out * theirs_rows
        top = joint
        step *= 2
    return (top.reshape(block_max.shape), total.reshape(block_sum.shape), out2.reshape(head_shape))


def on_device(
    tokens,
    cache_keys,
    cache_values,
    held_states,
    recompute_pos,
    cache_len,
    new_prompt,
    w_qkv,
    qkv_bias,
    w_out,
    out_bias,
    attn_gain,
    attn_shift,
    w_up,
    up_bias,
    w_down,
    down_bias,
    ffn_gain,
    ffn_shift,
):
    local_width = w_qkv.shape[2]
    local_heads = local_width // HDIM
    requests = cache_keys.shape[0]
    block_len = cache_keys.shape[1]
    own_rows = tokens.shape[0]
    steps_count = tokens.shape[1]
    block_rows = lax.all_gather(tokens, "head", axis=0, tiled=True)
    triple = (
        jnp.einsum("rtd,kdc->rtkc", block_rows, w_qkv, preferred_element_type=jnp.float32)
        + qkv_bias
    )
    triple = triple.astype(jnp.bfloat16).reshape(
        block_rows.shape[0], block_rows.shape[1], 3 * local_width
    )
    gathered = jnp.concatenate([triple, block_rows], axis=2)
    head_shape = (requests, steps_count, local_heads, HDIM)
    queries = gathered[:, :, :local_width].reshape(head_shape)
    new_keys = gathered[:, :, local_width : 2 * local_width].reshape(head_shape)
    new_values = gathered[:, :, 2 * local_width : 3 * local_width].reshape(head_shape)
    fresh_keys = (
        jnp.einsum("rjd,dc->rjc", held_states, w_qkv[1], preferred_element_type=jnp.float32)
        + qkv_bias[1]
    ).astype(jnp.bfloat16)
    offset_pos = lax.axis_index("seq") * block_len
    positions = jnp.arange(block_len, dtype=jnp.int32)
    matches = (recompute_pos - offset_pos)[:, :, None] == positions[None, None, :]
    placed = jnp.einsum(
        "rjp,rjc->rpc", matches.astype(jnp.bfloat16), fresh_keys, preferred_element_type=jnp.float32
    ).astype(jnp.bfloat16)
    replaced = jnp.any(matches, axis=1)
    keys_here = jnp.where(replaced[:, :, None], placed, cache_keys).reshape(
        requests, block_len, local_heads, HDIM
    )
    values_here = cache_values.reshape(requests, block_len, local_heads, HDIM)
    visible = ((offset_pos + positions)[None, :] < cache_len[:, None]) & (new_prompt[:, None] == 0)
    block_max, block_sum, block_out = partial_attention(
        queries, keys_here, values_here, visible[:, None, None, :]
    )
    cache_max, cache_sum, cache_out = seq_merge(block_max, block_sum, block_out)
    order_t = jnp.arange(steps_count, dtype=jnp.int32)
    causal = (order_t[:, None] >= order_t[None, :])[None, :, None, :]
    new_max, new_sum, new_out = partial_attention(queries, new_keys, new_values, causal)
    joint_max, joint_sum, joint_out = merge_pair(
        (cache_max, cache_sum, cache_out), (new_max, new_sum, new_out)
    )
    attended = (
        (joint_out / joint_sum[..., None])
        .astype(jnp.bfloat16)
        .reshape(requests, steps_count, local_width)
    )
    head_terms = jnp.einsum("rtc,cd->rtd", attended, w_out, preferred_element_type=jnp.float32)
    summed = lax.psum(head_terms, "head")
    inputs_all = gathered[:, :, 3 * local_width :]
    normed_all = layer_norm(
        inputs_all.astype(jnp.float32) + summed + out_bias, attn_gain, attn_shift
    ).astype(jnp.bfloat16)
    hidden_all = jax.nn.gelu(
        jnp.einsum("rtd,df->rtf", normed_all, w_up, preferred_element_type=jnp.float32) + up_bias,
        approximate=False,
    ).astype(jnp.bfloat16)
    normed = lax.dynamic_slice_in_dim(normed_all, lax.axis_index("head") * own_rows, own_rows, 0)
    reduced = lax.psum_scatter(
        jnp.einsum("rtf,fd->rtd", hidden_all, w_down, preferred_element_type=jnp.float32),
        "head",
        scatter_dimension=0,
        tiled=True,
    )
    return layer_norm(normed.astype(jnp.float32) + reduced + down_bias, ffn_gain, ffn_shift).astype(
        jnp.bfloat16
    )


def solution(mesh):
    placed = (
        P("head", None, None),
        P(None, "seq", "head"),
        P(None, "seq", "head"),
        P(None, "seq", None),
        P(None, "seq"),
        P(),
        P(),
        P(None, None, "head"),
        P(None, "head"),
        P("head", None),
        P(),
        P(),
        P(),
        P(None, "head"),
        P("head"),
        P("head", None),
        P(),
        P(),
        P(),
    )
    return jax.shard_map(
        on_device, mesh=mesh, in_specs=placed, out_specs=P("head", None, None), check_vma=False
    )
```

profile of v0, /device:TPU:8, one launch (start us, length us, event | category | flops | bytes accessed | tf_op | source)
XLA Modules:
  0.0 232.6 jit_solution(7463980318247415298)
XLA Ops:
  6.5 0.8 broadcast_compare_fusion
  7.3 0.7 slice_bitcast_fusion
  8.0 0.7 broadcast_subtract_fusion
  9.0 1.0 copy.122
  10.0 13.1 %all_gather.3 = bf16[64,4,1024]{2,0,1:T(8,128)(2,1)S(1)} all-gather(bf16[16,4,1024]{2,0,1:T(8,128)(2,1)S(1)} %copy.122), channel_id=1, replica_groups=mesh['seq'=128,'head'=4] {'head'}, dimensions={0}, use_global_device_ids=true | all-gather | bytes 655360 | tf_op jit(solution)/shard_map/all_gather | solution.py:101
  24.3 0.8 reshape.249
  25.3 0.7 copy-done.18
  26.1 0.9 fusion
  27.7 1.7 select_reduce_fusion
  32.4 1.9 collective-permute-start
  34.3 1.3 collective-permute-done
  36.4 3.8 %collective-permute-start.1 = (f32[264,128]{1,0:T(8,128)S(1)}, f32[264,128]{1,0:T(8,128)S(1)}, u32[]{:S(2)}, u32[]{:S(2)}) collective-permute-start(f32[264,128]{1,0:T(8,128)S(1)} %pad_maximum_fusion.1), channel_id=1, source_target_pairs={{0,8},{4,12},{8,0},{12,4},{16,24},{20,28},{24,16},{28,20},{32,40},... | collective-permute-start | bytes 405512 | tf_op jit(solution)/shard_map/ppermute | solution.py:58
  40.3 3.9 %collective-permute-done.1 = f32[264,128]{1,0:T(8,128)S(1)} collective-permute-done((f32[264,128]{1,0:T(8,128)S(1)}, f32[264,128]{1,0:T(8,128)S(1)}, u32[]{:S(2)}, u32[]{:S(2)}) %collective-permute-start.1) | collective-permute-done | bytes 135200 | tf_op jit(solution)/shard_map/ppermute | solution.py:58
  44.9 5.2 %collective-permute-start.2 = (f32[264,128]{1,0:T(8,128)S(1)}, f32[264,128]{1,0:T(8,128)S(1)}, u32[]{:S(2)}, u32[]{:S(2)}) collective-permute-start(f32[264,128]{1,0:T(8,128)S(1)} %pad_maximum_fusion.2), channel_id=1, source_target_pairs={{0,16},{4,20},{8,24},{12,28},{16,0},{20,4},{24,8},{28,12},{32,48},... | collective-permute-start | bytes 405512 | tf_op jit(solution)/shard_map/ppermute | solution.py:58
  50.1 6.1 %collective-permute-done.2 = f32[264,128]{1,0:T(8,128)S(1)} collective-permute-done((f32[264,128]{1,0:T(8,128)S(1)}, f32[264,128]{1,0:T(8,128)S(1)}, u32[]{:S(2)}, u32[]{:S(2)}) %collective-permute-start.2) | collective-permute-done | bytes 135200 | tf_op jit(solution)/shard_map/ppermute | solution.py:58
  57.0 9.1 %collective-permute-start.3 = (f32[264,128]{1,0:T(8,128)S(1)}, f32[264,128]{1,0:T(8,128)S(1)}, u32[]{:S(2)}, u32[]{:S(2)}) collective-permute-start(f32[264,128]{1,0:T(8,128)S(1)} %pad_maximum_fusion.3), channel_id=1, source_target_pairs={{0,32},{4,36},{8,40},{12,44},{16,48},{20,52},{24,56},{28,60},{32,0... | collective-permute-start | bytes 405512 | tf_op jit(solution)/shard_map/ppermute | solution.py:58
  66.2 10.2 %collective-permute-done.3 = f32[264,128]{1,0:T(8,128)S(1)} collective-permute-done((f32[264,128]{1,0:T(8,128)S(1)}, f32[264,128]{1,0:T(8,128)S(1)}, u32[]{:S(2)}, u32[]{:S(2)}) %collective-permute-start.3) | collective-permute-done | bytes 135200 | tf_op jit(solution)/shard_map/ppermute | solution.py:58
  77.1 13.6 %collective-permute-start.4 = (f32[264,128]{1,0:T(8,128)S(1)}, f32[264,128]{1,0:T(8,128)S(1)}, u32[]{:S(2)}, u32[]{:S(2)}) collective-permute-start(f32[264,128]{1,0:T(8,128)S(1)} %pad_maximum_fusion.4), channel_id=1, source_target_pairs={{0,64},{4,68},{8,72},{12,76},{16,80},{20,84},{24,88},{28,92},{32,9... | collective-permute-start | bytes 405512 | tf_op jit(solution)/shard_map/ppermute | solution.py:58
  91.0 12.1 %collective-permute-done.4 = f32[264,128]{1,0:T(8,128)S(1)} collective-permute-done((f32[264,128]{1,0:T(8,128)S(1)}, f32[264,128]{1,0:T(8,128)S(1)}, u32[]{:S(2)}, u32[]{:S(2)}) %collective-permute-start.4) | collective-permute-done | bytes 135200 | tf_op jit(solution)/shard_map/ppermute | solution.py:58
  103.9 3.5 %collective-permute-start.5 = (f32[264,128]{1,0:T(8,128)S(1)}, f32[264,128]{1,0:T(8,128)S(1)}, u32[]{:S(2)}, u32[]{:S(2)}) collective-permute-start(f32[264,128]{1,0:T(8,128)S(1)} %pad_maximum_fusion.5), channel_id=1, source_target_pairs={{0,128},{4,132},{8,136},{12,140},{16,144},{20,148},{24,152},{28,15... | collective-permute-start | bytes 405512 | tf_op jit(solution)/shard_map/ppermute | solution.py:58
  107.8 3.3 %collective-permute-done.5 = f32[264,128]{1,0:T(8,128)S(1)} collective-permute-done((f32[264,128]{1,0:T(8,128)S(1)}, f32[264,128]{1,0:T(8,128)S(1)}, u32[]{:S(2)}, u32[]{:S(2)}) %collective-permute-start.5) | collective-permute-done | bytes 135200 | tf_op jit(solution)/shard_map/ppermute | solution.py:58
  111.9 3.9 %collective-permute-start.6 = (f32[264,128]{1,0:T(8,128)S(1)}, f32[264,128]{1,0:T(8,128)S(1)}, u32[]{:S(2)}, u32[]{:S(2)}) collective-permute-start(f32[264,128]{1,0:T(8,128)S(1)} %pad_maximum_fusion.6), channel_id=1, source_target_pairs={{0,256},{4,260},{8,264},{12,268},{16,272},{20,276},{24,280},{28,28... | collective-permute-start | bytes 405512 | tf_op jit(solution)/shard_map/ppermute | solution.py:58
  116.1 4.2 %collective-permute-done.6 = f32[264,128]{1,0:T(8,128)S(1)} collective-permute-done((f32[264,128]{1,0:T(8,128)S(1)}, f32[264,128]{1,0:T(8,128)S(1)}, u32[]{:S(2)}, u32[]{:S(2)}) %collective-permute-start.6) | collective-permute-done | bytes 135200 | tf_op jit(solution)/shard_map/ppermute | solution.py:58
  123.0 0.7 copy-done.6
  123.7 1.3 fusion.29
  125.3 58.1 %all-reduce.2.cloned.1.call-done = f32[64,4,1024]{2,0,1:T(8,128)} async-done(((f32[64,4,1024]{2,0,1:T(8,128)}), f32[64,4,1024]{2,0,1:T(8,128)}) %all-reduce.2.cloned.1.call-update) | async-done | bytes 1048592 | tf_op jit(solution)/shard_map/psum | solution.py:146
  183.4 1.5 fusion.26
  186.3 0.9 copy-done.16
  187.8 2.5 %fusion.9 = f32[64,4,1024]{2,0,1:T(8,128)} fusion(bf16[512,1024]{1,0:T(8,128)(2,1)S(1)} %copy-done, f32[64,4,512]{2,0,1:T(8,128)S(1)} %get-tuple-element.45, u8[64,512]{1,0:T(8,128)(4,1)S(1)} %get-tuple-element.6, u8[64,512]{1,0:T(8,128)(4,1)S(1)} %get-tuple-element.5), kind=kOutput, calls=%fused_computation.16 | convolution fusion | flops 277610496 | bytes 2686976 | tf_op jit(solution)/shard_map/rtf,fd->rtd/dot_general | solution.py:157
  190.3 32.6 %reduce-scatter.2.cloned.1.call-done = f32[16,4,1024]{2,0,1:T(8,128)} async-done(((f32[64,4,1024]{2,0,1:T(8,128)}), f32[16,4,1024]{2,0,1:T(8,128)}) %reduce-scatter.2.cloned.1.call-update) | async-done | bytes 262160 | tf_op jit(solution)/shard_map/reduce_scatter | solution.py:156
  222.9 1.1 fusion.82
  225.0 0.8 copy.180
  (165 shorter events, 16.3 us)
Async XLA Ops:
  6.5 181.2 %copy-start = (bf16[512,1024]{1,0:T(8,128)(2,1)S(1)}, bf16[512,1024]{1,0:T(8,128)(2,1)}, u32[]{:S(2)}) copy-start(bf16[512,1024]{1,0:T(8,128)(2,1)} %param.34) | copy-start | bytes 3145732
  6.5 16.6 %copy-start.3 = (bf16[3,1024,128]{2,1,0:T(8,128)(2,1)S(1)}, bf16[3,1024,128]{2,1,0:T(8,128)(2,1)}, u32[]{:S(2)}) copy-start(bf16[3,1024,128]{2,1,0:T(8,128)(2,1)} %param.26) | copy-start | bytes 2359300
  6.5 176.9 %all-reduce.2.cloned.1.call-start = ((), (), s32[]{:S(2)}) async-start(), calls=%async_computation.1 | async-start | bytes 2097152 | tf_op jit(solution)/shard_map/psum | solution.py:146
  9.9 13.2 %copy-start.14 = (f32[3,128]{1,0:T(4,128)S(1)}, f32[3,128]{1,0:T(4,128)}, u32[]{:S(2)}) copy-start(f32[3,128]{1,0:T(4,128)} %param.27) | copy-start | bytes 4612
  23.5 1.5 copy-start.17
  25.0 1.0 copy-start.18
  27.0 0.7 copy-start.15
  29.4 1.8 copy-start.4
  32.4 3.2 %collective-permute-start = (f32[264,128]{1,0:T(8,128)S(1)}, f32[264,128]{1,0:T(8,128)S(1)}, u32[]{:S(2)}, u32[]{:S(2)}) collective-permute-start(f32[264,128]{1,0:T(8,128)S(1)} %pad_maximum_fusion), channel_id=1, source_target_pairs={{0,4},{4,0},{8,12},{12,8},{16,20},{20,16},{24,28},{28,24},{32,36},... | collective-permute-start | bytes 405512 | tf_op jit(solution)/shard_map/ppermute | solution.py:58
  36.4 7.7 %collective-permute-start.1 = (f32[264,128]{1,0:T(8,128)S(1)}, f32[264,128]{1,0:T(8,128)S(1)}, u32[]{:S(2)}, u32[]{:S(2)}) collective-permute-start(f32[264,128]{1,0:T(8,128)S(1)} %pad_maximum_fusion.1), channel_id=1, source_target_pairs={{0,8},{4,12},{8,0},{12,4},{16,24},{20,28},{24,16},{28,20},{32,40},... | collective-permute-start | bytes 405512 | tf_op jit(solution)/shard_map/ppermute | solution.py:58
  44.9 11.3 %collective-permute-start.2 = (f32[264,128]{1,0:T(8,128)S(1)}, f32[264,128]{1,0:T(8,128)S(1)}, u32[]{:S(2)}, u32[]{:S(2)}) collective-permute-start(f32[264,128]{1,0:T(8,128)S(1)} %pad_maximum_fusion.2), channel_id=1, source_target_pairs={{0,16},{4,20},{8,24},{12,28},{16,0},{20,4},{24,8},{28,12},{32,48},... | collective-permute-start | bytes 405512 | tf_op jit(solution)/shard_map/ppermute | solution.py:58
  56.9 9.1 %copy-start.5 = (bf16[64,4,128]{2,0,1:T(8,128)(2,1)S(1)}, bf16[64,4,128]{2,0,1:T(8,128)(2,1)}, u32[]{:S(2)}) copy-start(bf16[64,4,128]{2,0,1:T(8,128)(2,1)} %get-tuple-element.41) | copy-start | bytes 196612
  57.0 19.4 %collective-permute-start.3 = (f32[264,128]{1,0:T(8,128)S(1)}, f32[264,128]{1,0:T(8,128)S(1)}, u32[]{:S(2)}, u32[]{:S(2)}) collective-permute-start(f32[264,128]{1,0:T(8,128)S(1)} %pad_maximum_fusion.3), channel_id=1, source_target_pairs={{0,32},{4,36},{8,40},{12,44},{16,48},{20,52},{24,56},{28,60},{32,0... | collective-permute-start | bytes 405512 | tf_op jit(solution)/shard_map/ppermute | solution.py:58
  77.1 13.6 %copy-start.7 = (bf16[64,4,2,64]{3,2,0,1:T(2,128)(2,1)S(1)}, bf16[64,4,2,64]{3,2,0,1:T(2,128)(2,1)}, u32[]{:S(2)}) copy-start(bf16[64,4,2,64]{3,2,0,1:T(2,128)(2,1)} %reshape.249) | copy-start | bytes 196612
  77.1 26.0 %collective-permute-start.4 = (f32[264,128]{1,0:T(8,128)S(1)}, f32[264,128]{1,0:T(8,128)S(1)}, u32[]{:S(2)}, u32[]{:S(2)}) collective-permute-start(f32[264,128]{1,0:T(8,128)S(1)} %pad_maximum_fusion.4), channel_id=1, source_target_pairs={{0,64},{4,68},{8,72},{12,76},{16,80},{20,84},{24,88},{28,92},{32,9... | collective-permute-start | bytes 405512 | tf_op jit(solution)/shard_map/ppermute | solution.py:58
  103.9 7.2 %collective-permute-start.5 = (f32[264,128]{1,0:T(8,128)S(1)}, f32[264,128]{1,0:T(8,128)S(1)}, u32[]{:S(2)}, u32[]{:S(2)}) collective-permute-start(f32[264,128]{1,0:T(8,128)S(1)} %pad_maximum_fusion.5), channel_id=1, source_target_pairs={{0,128},{4,132},{8,136},{12,140},{16,144},{20,148},{24,152},{28,15... | collective-permute-start | bytes 405512 | tf_op jit(solution)/shard_map/ppermute | solution.py:58
  111.9 8.4 %collective-permute-start.6 = (f32[264,128]{1,0:T(8,128)S(1)}, f32[264,128]{1,0:T(8,128)S(1)}, u32[]{:S(2)}, u32[]{:S(2)}) collective-permute-start(f32[264,128]{1,0:T(8,128)S(1)} %pad_maximum_fusion.6), channel_id=1, source_target_pairs={{0,256},{4,260},{8,264},{12,268},{16,272},{20,276},{24,280},{28,28... | collective-permute-start | bytes 405512 | tf_op jit(solution)/shard_map/ppermute | solution.py:58
  122.8 1.0 copy-start.6
  125.1 58.4 %copy-start.8 = (f32[1024]{0:T(1024)S(1)}, f32[1024]{0:T(1024)}, u32[]{:S(2)}) copy-start(f32[1024]{0:T(1024)} %param.29) | copy-start | bytes 12292
  125.1 97.8 %reduce-scatter.2.cloned.1.call-start = ((), (), s32[]{:S(2)}) async-start(), calls=%async_computation.2 | async-start | bytes 1310720 | tf_op jit(solution)/shard_map/reduce_scatter | solution.py:156
  183.4 1.5 copy-start.1
  185.0 0.7 copy-start.11
  185.3 0.7 copy-start.10
  186.0 1.2 copy-start.16
  186.0 1.2 copy-start.19
  190.3 32.6 %copy-start.9 = (f32[1024]{0:T(1024)S(1)}, f32[1024]{0:T(1024)}, u32[]{:S(2)}) copy-start(f32[1024]{0:T(1024)} %param.35) | copy-start | bytes 12292
  222.9 1.1 copy-start.2
  222.9 1.4 copy-start.13
  224.2 0.7 copy-start.12
Sparse Core Ops, SparseCore 0:
  125.2 58.1 all-reduce.1
  190.4 32.4 reduce-scatter.1
where the time goes:
time: 233 us
  waiting for transfers between devices  132 us (57%)
  starting transfers between devices  41.2 us (18%)
  local copies, waits for them, and re-layouts  16.8 us (7%)
  between operations  14.3 us (6%)
  blocking collectives  13.1 us (6%)
  matrix products  8.92 us (4%)
  other arithmetic  6.39 us (3%)
    psum x1, waiting for transfers between devices, on_device(): summed = lax.psum(head_terms, 'head')  58.1 us
    ppermute x7, waiting for transfers between devices, seq_merge(): other = lax.ppermute(packed, 'seq', pairs)  41.2 us
    ppermute x7, starting transfers between devices, seq_merge(): other = lax.ppermute(packed, 'seq', pairs)  41 us
    reduce_scatter x1, waiting for transfers between devices, on_device(): lax.psum_scatter(jnp.einsum('rtf,fd->rtd', hidden_all, w_down, preferred_...  32.6 us
    all_gather x1, blocking collectives, on_device(): block_rows = lax.all_gather(tokens, 'head', axis=0, tiled=True)  13.1 us
    unnamed x41, local copies, waits for them, and re-layouts  4.99 us
  transfers between devices with their start and end apart: 9, of which 9 were waited for; matrix products, arithmetic and copies ran while one was open for 0% of the time, Pallas kernels for 0%

commit v1 on v0

--- a/solution.py
+++ b/solution.py
@@ -143,7 +143,9 @@
         .reshape(requests, steps_count, local_width)
     )
     head_terms = jnp.einsum("rtc,cd->rtd", attended, w_out, preferred_element_type=jnp.float32)
-    summed = lax.psum(head_terms, "head")
+    summed = head_terms
+    for hop in (1, 2):
+        summed = summed + lax.ppermute(summed, "head", [(dev, dev ^ hop) for dev in range(4)])
     inputs_all = gathered[:, :, 3 * local_width :]
     normed_all = layer_norm(
         inputs_all.astype(jnp.float32) + summed + out_bias, attn_gain, attn_shift

time: 233 us -> 219 us (0.940)
  waiting for transfers between devices: 132 us -> 113 us
  starting transfers between devices: 41.2 us -> 48.2 us
    psum x1 -> x0, waiting for transfers between devices: 58.1 us -> none  [on_device(): summed = lax.psum(head_terms, 'head')]
    ppermute x0 -> x2, waiting for transfers between devices: none -> 43.1 us  [on_device(): lax.ppermute(summed, 'head', [(dev, dev ^ hop) for dev in range(4)])]
    ppermute x0 -> x2, starting transfers between devices: none -> 7.16 us  [on_device(): lax.ppermute(summed, 'head', [(dev, dev ^ hop) for dev in range(4)])]
    reduce_scatter x1, waiting for transfers between devices: 32.6 us -> 28.5 us  [on_device(): lax.psum_scatter(jnp.einsum('rtf,fd->rtd', hidden_all, w_down, preferred_...]
    unnamed x41 -> x39, local copies, waits for them, and re-layouts: 4.99 us -> 4.53 us
  transfers between devices with their start and end apart: 9 -> 10, of which waited for: 9 -> 10; matrix products, arithmetic and copies ran while one was open for 0% -> 0% of each run, Pallas kernels for 0% -> 0%
where the time goes in v1:
time: 219 us; the launch traced here: 218 us
  waiting for transfers between devices  113 us (52%)
  starting transfers between devices  48.2 us (22%)
  local copies, waits for them, and re-layouts  16.4 us (7%)
  between operations  14.3 us (7%)
  blocking collectives  13.1 us (6%)
  matrix products  7.9 us (4%)
  other arithmetic  5.2 us (2%)
    ppermute x2, waiting for transfers between devices, on_device(): lax.ppermute(summed, 'head', [(dev, dev ^ hop) for dev in range(4)])  43.1 us
    ppermute x7, waiting for transfers between devices, seq_merge(): other = lax.ppermute(packed, 'seq', pairs)  41.2 us
    ppermute x7, starting transfers between devices, seq_merge(): other = lax.ppermute(packed, 'seq', pairs)  41 us
    reduce_scatter x1, waiting for transfers between devices, on_device(): lax.psum_scatter(jnp.einsum('rtf,fd->rtd', hidden_all, w_down, preferred_...  28.5 us
    all_gather x1, blocking collectives, on_device(): block_rows = lax.all_gather(tokens, 'head', axis=0, tiled=True)  13.1 us
    ppermute x2, starting transfers between devices, on_device(): lax.ppermute(summed, 'head', [(dev, dev ^ hop) for dev in range(4)])  7.16 us
    unnamed x39, local copies, waits for them, and re-layouts  4.53 us
  transfers between devices with their start and end apart: 10, of which 10 were waited for; matrix products, arithmetic and copies ran while one was open for 0% of the time, Pallas kernels for 0%

profile of v1, /device:TPU:8, one launch (start us, length us, event | category | flops | bytes accessed | tf_op | source)
XLA Modules:
  0.0 217.9 jit_solution(17954690829291659920)
XLA Ops:
  6.5 0.8 broadcast_compare_fusion
  7.3 0.7 slice_bitcast_fusion
  8.0 0.7 broadcast_subtract_fusion
  9.0 1.0 copy.122
  10.0 13.1 %all_gather.3 = bf16[64,4,1024]{2,0,1:T(8,128)(2,1)S(1)} all-gather(bf16[16,4,1024]{2,0,1:T(8,128)(2,1)S(1)} %copy.122), channel_id=1, replica_groups=mesh['seq'=128,'head'=4] {'head'}, dimensions={0}, use_global_device_ids=true | all-gather | bytes 655360 | tf_op jit(solution)/shard_map/all_gather | solution.py:101
  24.3 0.8 reshape.249
  25.3 0.7 copy-done.17
  26.1 0.9 fusion
  27.7 1.7 select_reduce_fusion
  32.4 1.9 collective-permute-start
  34.3 1.3 collective-permute-done
  36.4 3.8 %collective-permute-start.1 = (f32[264,128]{1,0:T(8,128)S(1)}, f32[264,128]{1,0:T(8,128)S(1)}, u32[]{:S(2)}, u32[]{:S(2)}) collective-permute-start(f32[264,128]{1,0:T(8,128)S(1)} %pad_maximum_fusion.1), channel_id=1, source_target_pairs={{0,8},{4,12},{8,0},{12,4},{16,24},{20,28},{24,16},{28,20},{32,40},... | collective-permute-start | bytes 405512 | tf_op jit(solution)/shard_map/ppermute | solution.py:58
  40.3 3.9 %collective-permute-done.1 = f32[264,128]{1,0:T(8,128)S(1)} collective-permute-done((f32[264,128]{1,0:T(8,128)S(1)}, f32[264,128]{1,0:T(8,128)S(1)}, u32[]{:S(2)}, u32[]{:S(2)}) %collective-permute-start.1) | collective-permute-done | bytes 135200 | tf_op jit(solution)/shard_map/ppermute | solution.py:58
  44.9 5.2 %collective-permute-start.2 = (f32[264,128]{1,0:T(8,128)S(1)}, f32[264,128]{1,0:T(8,128)S(1)}, u32[]{:S(2)}, u32[]{:S(2)}) collective-permute-start(f32[264,128]{1,0:T(8,128)S(1)} %pad_maximum_fusion.2), channel_id=1, source_target_pairs={{0,16},{4,20},{8,24},{12,28},{16,0},{20,4},{24,8},{28,12},{32,48},... | collective-permute-start | bytes 405512 | tf_op jit(solution)/shard_map/ppermute | solution.py:58
  50.1 6.1 %collective-permute-done.2 = f32[264,128]{1,0:T(8,128)S(1)} collective-permute-done((f32[264,128]{1,0:T(8,128)S(1)}, f32[264,128]{1,0:T(8,128)S(1)}, u32[]{:S(2)}, u32[]{:S(2)}) %collective-permute-start.2) | collective-permute-done | bytes 135200 | tf_op jit(solution)/shard_map/ppermute | solution.py:58
  57.0 9.1 %collective-permute-start.3 = (f32[264,128]{1,0:T(8,128)S(1)}, f32[264,128]{1,0:T(8,128)S(1)}, u32[]{:S(2)}, u32[]{:S(2)}) collective-permute-start(f32[264,128]{1,0:T(8,128)S(1)} %pad_maximum_fusion.3), channel_id=1, source_target_pairs={{0,32},{4,36},{8,40},{12,44},{16,48},{20,52},{24,56},{28,60},{32,0... | collective-permute-start | bytes 405512 | tf_op jit(solution)/shard_map/ppermute | solution.py:58
  66.2 10.2 %collective-permute-done.3 = f32[264,128]{1,0:T(8,128)S(1)} collective-permute-done((f32[264,128]{1,0:T(8,128)S(1)}, f32[264,128]{1,0:T(8,128)S(1)}, u32[]{:S(2)}, u32[]{:S(2)}) %collective-permute-start.3) | collective-permute-done | bytes 135200 | tf_op jit(solution)/shard_map/ppermute | solution.py:58
  77.1 13.6 %collective-permute-start.4 = (f32[264,128]{1,0:T(8,128)S(1)}, f32[264,128]{1,0:T(8,128)S(1)}, u32[]{:S(2)}, u32[]{:S(2)}) collective-permute-start(f32[264,128]{1,0:T(8,128)S(1)} %pad_maximum_fusion.4), channel_id=1, source_target_pairs={{0,64},{4,68},{8,72},{12,76},{16,80},{20,84},{24,88},{28,92},{32,9... | collective-permute-start | bytes 405512 | tf_op jit(solution)/shard_map/ppermute | solution.py:58
  91.0 12.1 %collective-permute-done.4 = f32[264,128]{1,0:T(8,128)S(1)} collective-permute-done((f32[264,128]{1,0:T(8,128)S(1)}, f32[264,128]{1,0:T(8,128)S(1)}, u32[]{:S(2)}, u32[]{:S(2)}) %collective-permute-start.4) | collective-permute-done | bytes 135200 | tf_op jit(solution)/shard_map/ppermute | solution.py:58
  103.9 3.5 %collective-permute-start.5 = (f32[264,128]{1,0:T(8,128)S(1)}, f32[264,128]{1,0:T(8,128)S(1)}, u32[]{:S(2)}, u32[]{:S(2)}) collective-permute-start(f32[264,128]{1,0:T(8,128)S(1)} %pad_maximum_fusion.5), channel_id=1, source_target_pairs={{0,128},{4,132},{8,136},{12,140},{16,144},{20,148},{24,152},{28,15... | collective-permute-start | bytes 405512 | tf_op jit(solution)/shard_map/ppermute | solution.py:58
  107.8 3.3 %collective-permute-done.5 = f32[264,128]{1,0:T(8,128)S(1)} collective-permute-done((f32[264,128]{1,0:T(8,128)S(1)}, f32[264,128]{1,0:T(8,128)S(1)}, u32[]{:S(2)}, u32[]{:S(2)}) %collective-permute-start.5) | collective-permute-done | bytes 135200 | tf_op jit(solution)/shard_map/ppermute | solution.py:58
  111.9 3.9 %collective-permute-start.6 = (f32[264,128]{1,0:T(8,128)S(1)}, f32[264,128]{1,0:T(8,128)S(1)}, u32[]{:S(2)}, u32[]{:S(2)}) collective-permute-start(f32[264,128]{1,0:T(8,128)S(1)} %pad_maximum_fusion.6), channel_id=1, source_target_pairs={{0,256},{4,260},{8,264},{12,268},{16,272},{20,276},{24,280},{28,28... | collective-permute-start | bytes 405512 | tf_op jit(solution)/shard_map/ppermute | solution.py:58
  116.1 4.2 %collective-permute-done.6 = f32[264,128]{1,0:T(8,128)S(1)} collective-permute-done((f32[264,128]{1,0:T(8,128)S(1)}, f32[264,128]{1,0:T(8,128)S(1)}, u32[]{:S(2)}, u32[]{:S(2)}) %collective-permute-start.6) | collective-permute-done | bytes 135200 | tf_op jit(solution)/shard_map/ppermute | solution.py:58
  123.0 0.7 copy-done.5
  124.0 3.4 %collective-permute-start.7 = (f32[64,4,1024]{2,0,1:T(8,128)S(1)}, f32[64,4,1024]{2,0,1:T(8,128)S(1)}, u32[]{:S(2)}, u32[]{:S(2)}) collective-permute-start(f32[64,4,1024]{2,0,1:T(8,128)S(1)} %fusion.28), channel_id=1, source_target_pairs={{0,1},{1,0},{2,3},{3,2},{4,5},{5,4},{6,7},{7,6},{8,9},{9,8},{10,11... | collective-permute-start | bytes 3145736 | tf_op jit(solution)/shard_map/ppermute | solution.py:148
  127.4 21.4 %collective-permute-done.7 = f32[64,4,1024]{2,0,1:T(8,128)S(1)} collective-permute-done((f32[64,4,1024]{2,0,1:T(8,128)S(1)}, f32[64,4,1024]{2,0,1:T(8,128)S(1)}, u32[]{:S(2)}, u32[]{:S(2)}) %collective-permute-start.7) | collective-permute-done | bytes 1048608 | tf_op jit(solution)/shard_map/ppermute | solution.py:148
  149.0 3.8 %collective-permute-start.8 = (f32[64,4,1024]{2,0,1:T(8,128)S(1)}, f32[64,4,1024]{2,0,1:T(8,128)S(1)}, u32[]{:S(2)}, u32[]{:S(2)}) collective-permute-start(f32[64,4,1024]{2,0,1:T(8,128)S(1)} %add.182), channel_id=1, source_target_pairs={{0,2},{1,3},{2,0},{3,1},{4,6},{5,7},{6,4},{7,5},{8,10},{9,11},{10,... | collective-permute-start | bytes 3145736 | tf_op jit(solution)/shard_map/ppermute | solution.py:148
  152.8 21.7 %collective-permute-done.8 = f32[64,4,1024]{2,0,1:T(8,128)S(1)} collective-permute-done((f32[64,4,1024]{2,0,1:T(8,128)S(1)}, f32[64,4,1024]{2,0,1:T(8,128)S(1)}, u32[]{:S(2)}, u32[]{:S(2)}) %collective-permute-start.8) | collective-permute-done | bytes 1048608 | tf_op jit(solution)/shard_map/ppermute | solution.py:148
  177.0 2.5 %fusion.9 = f32[64,4,1024]{2,0,1:T(8,128)} fusion(bf16[512,1024]{1,0:T(8,128)(2,1)S(1)} %copy-done, f32[64,4,512]{2,0,1:T(8,128)S(1)} %get-tuple-element.47, u8[64,512]{1,0:T(8,128)(4,1)S(1)} %get-tuple-element.6, u8[64,512]{1,0:T(8,128)(4,1)S(1)} %get-tuple-element.5), kind=kOutput, calls=%fused_computation.16 | convolution fusion | flops 277610496 | bytes 2686976 | tf_op jit(solution)/shard_map/rtf,fd->rtd/dot_general | solution.py:159
  179.6 28.5 %reduce-scatter.2.cloned.1.call-done = f32[16,4,1024]{2,0,1:T(8,128)} async-done(((f32[64,4,1024]{2,0,1:T(8,128)}), f32[16,4,1024]{2,0,1:T(8,128)}) %reduce-scatter.2.cloned.1.call-update) | async-done | bytes 262160 | tf_op jit(solution)/shard_map/reduce_scatter | solution.py:158
  208.1 1.1 fusion.81
  210.2 0.8 copy.180
  (165 shorter events, 17.2 us)
Async XLA Ops:
  6.5 170.5 %copy-start = (bf16[512,1024]{1,0:T(8,128)(2,1)S(1)}, bf16[512,1024]{1,0:T(8,128)(2,1)}, u32[]{:S(2)}) copy-start(bf16[512,1024]{1,0:T(8,128)(2,1)} %param.34) | copy-start | bytes 3145732
  6.5 16.6 %copy-start.2 = (bf16[3,1024,128]{2,1,0:T(8,128)(2,1)S(1)}, bf16[3,1024,128]{2,1,0:T(8,128)(2,1)}, u32[]{:S(2)}) copy-start(bf16[3,1024,128]{2,1,0:T(8,128)(2,1)} %param.26) | copy-start | bytes 2359300
  6.5 201.6 %reduce-scatter.2.cloned.1.call-start = ((), (), s32[]{:S(2)}) async-start(), calls=%async_computation.1 | async-start | bytes 1310720 | tf_op jit(solution)/shard_map/reduce_scatter | solution.py:158
  9.9 13.2 %copy-start.13 = (f32[3,128]{1,0:T(4,128)S(1)}, f32[3,128]{1,0:T(4,128)}, u32[]{:S(2)}) copy-start(f32[3,128]{1,0:T(4,128)} %param.27) | copy-start | bytes 4612
  23.5 1.5 copy-start.16
  25.0 1.0 copy-start.17
  27.0 0.7 copy-start.14
  29.4 1.8 copy-start.3
  32.4 3.2 %collective-permute-start = (f32[264,128]{1,0:T(8,128)S(1)}, f32[264,128]{1,0:T(8,128)S(1)}, u32[]{:S(2)}, u32[]{:S(2)}) collective-permute-start(f32[264,128]{1,0:T(8,128)S(1)} %pad_maximum_fusion), channel_id=1, source_target_pairs={{0,4},{4,0},{8,12},{12,8},{16,20},{20,16},{24,28},{28,24},{32,36},... | collective-permute-start | bytes 405512 | tf_op jit(solution)/shard_map/ppermute | solution.py:58
  36.4 7.7 %collective-permute-start.1 = (f32[264,128]{1,0:T(8,128)S(1)}, f32[264,128]{1,0:T(8,128)S(1)}, u32[]{:S(2)}, u32[]{:S(2)}) collective-permute-start(f32[264,128]{1,0:T(8,128)S(1)} %pad_maximum_fusion.1), channel_id=1, source_target_pairs={{0,8},{4,12},{8,0},{12,4},{16,24},{20,28},{24,16},{28,20},{32,40},... | collective-permute-start | bytes 405512 | tf_op jit(solution)/shard_map/ppermute | solution.py:58
  44.9 11.3 %collective-permute-start.2 = (f32[264,128]{1,0:T(8,128)S(1)}, f32[264,128]{1,0:T(8,128)S(1)}, u32[]{:S(2)}, u32[]{:S(2)}) collective-permute-start(f32[264,128]{1,0:T(8,128)S(1)} %pad_maximum_fusion.2), channel_id=1, source_target_pairs={{0,16},{4,20},{8,24},{12,28},{16,0},{20,4},{24,8},{28,12},{32,48},... | collective-permute-start | bytes 405512 | tf_op jit(solution)/shard_map/ppermute | solution.py:58
  56.9 9.1 %copy-start.4 = (bf16[64,4,128]{2,0,1:T(8,128)(2,1)S(1)}, bf16[64,4,128]{2,0,1:T(8,128)(2,1)}, u32[]{:S(2)}) copy-start(bf16[64,4,128]{2,0,1:T(8,128)(2,1)} %get-tuple-element.43) | copy-start | bytes 196612
  57.0 19.4 %collective-permute-start.3 = (f32[264,128]{1,0:T(8,128)S(1)}, f32[264,128]{1,0:T(8,128)S(1)}, u32[]{:S(2)}, u32[]{:S(2)}) collective-permute-start(f32[264,128]{1,0:T(8,128)S(1)} %pad_maximum_fusion.3), channel_id=1, source_target_pairs={{0,32},{4,36},{8,40},{12,44},{16,48},{20,52},{24,56},{28,60},{32,0... | collective-permute-start | bytes 405512 | tf_op jit(solution)/shard_map/ppermute | solution.py:58
  77.1 13.6 %copy-start.6 = (bf16[64,4,2,64]{3,2,0,1:T(2,128)(2,1)S(1)}, bf16[64,4,2,64]{3,2,0,1:T(2,128)(2,1)}, u32[]{:S(2)}) copy-start(bf16[64,4,2,64]{3,2,0,1:T(2,128)(2,1)} %reshape.249) | copy-start | bytes 196612
  77.1 26.0 %collective-permute-start.4 = (f32[264,128]{1,0:T(8,128)S(1)}, f32[264,128]{1,0:T(8,128)S(1)}, u32[]{:S(2)}, u32[]{:S(2)}) collective-permute-start(f32[264,128]{1,0:T(8,128)S(1)} %pad_maximum_fusion.4), channel_id=1, source_target_pairs={{0,64},{4,68},{8,72},{12,76},{16,80},{20,84},{24,88},{28,92},{32,9... | collective-permute-start | bytes 405512 | tf_op jit(solution)/shard_map/ppermute | solution.py:58
  103.9 7.2 %collective-permute-start.5 = (f32[264,128]{1,0:T(8,128)S(1)}, f32[264,128]{1,0:T(8,128)S(1)}, u32[]{:S(2)}, u32[]{:S(2)}) collective-permute-start(f32[264,128]{1,0:T(8,128)S(1)} %pad_maximum_fusion.5), channel_id=1, source_target_pairs={{0,128},{4,132},{8,136},{12,140},{16,144},{20,148},{24,152},{28,15... | collective-permute-start | bytes 405512 | tf_op jit(solution)/shard_map/ppermute | solution.py:58
  111.9 8.4 %collective-permute-start.6 = (f32[264,128]{1,0:T(8,128)S(1)}, f32[264,128]{1,0:T(8,128)S(1)}, u32[]{:S(2)}, u32[]{:S(2)}) collective-permute-start(f32[264,128]{1,0:T(8,128)S(1)} %pad_maximum_fusion.6), channel_id=1, source_target_pairs={{0,256},{4,260},{8,264},{12,268},{16,272},{20,276},{24,280},{28,28... | collective-permute-start | bytes 405512 | tf_op jit(solution)/shard_map/ppermute | solution.py:58
  122.8 1.0 copy-start.5
  124.0 50.4 %copy-start.12 = (f32[1024]{0:T(1024)S(1)}, f32[1024]{0:T(1024)}, u32[]{:S(2)}) copy-start(f32[1024]{0:T(1024)} %param.29) | copy-start | bytes 12292
  124.0 24.8 %collective-permute-start.7 = (f32[64,4,1024]{2,0,1:T(8,128)S(1)}, f32[64,4,1024]{2,0,1:T(8,128)S(1)}, u32[]{:S(2)}, u32[]{:S(2)}) collective-permute-start(f32[64,4,1024]{2,0,1:T(8,128)S(1)} %fusion.28), channel_id=1, source_target_pairs={{0,1},{1,0},{2,3},{3,2},{4,5},{5,4},{6,7},{7,6},{8,9},{9,8},{10,11... | collective-permute-start | bytes 3145736 | tf_op jit(solution)/shard_map/ppermute | solution.py:148
  149.0 25.4 %collective-permute-start.8 = (f32[64,4,1024]{2,0,1:T(8,128)S(1)}, f32[64,4,1024]{2,0,1:T(8,128)S(1)}, u32[]{:S(2)}, u32[]{:S(2)}) collective-permute-start(f32[64,4,1024]{2,0,1:T(8,128)S(1)} %add.182), channel_id=1, source_target_pairs={{0,2},{1,3},{2,0},{3,1},{4,6},{5,7},{6,4},{7,5},{8,10},{9,11},{10,... | collective-permute-start | bytes 3145736 | tf_op jit(solution)/shard_map/ppermute | solution.py:148
  174.7 0.7 copy-start.9
  175.0 0.7 copy-start.8
  175.0 1.2 copy-start.15
  175.7 0.8 copy-start.18
  179.5 28.6 %copy-start.7 = (f32[1024]{0:T(1024)S(1)}, f32[1024]{0:T(1024)}, u32[]{:S(2)}) copy-start(f32[1024]{0:T(1024)} %param.35) | copy-start | bytes 12292
  208.1 1.1 copy-start.1
  208.1 1.4 copy-start.11
  209.4 0.7 copy-start.10
Sparse Core Ops, SparseCore 0:
  179.7 28.3 reduce-scatter.1
